TPU v7x, 256 devices: a whole 4x4x8 slice. The times are simulated.
256 devices in a mesh: band: 16 (over z_hi, y, core), grid: 16 (over x, z_lo).
Axes of the slice: x: 4, y: 4, z: 8 (z_hi: 2, z_lo: 4; z = z_hi * 4 + z_lo), core: 2. Of those that a mesh axis runs over, the one named last changes fastest.
Arguments:
- bands: float32 [16, 2, 128, 128, 128], P('band', None, 'grid'), may hold values from -6 to 6
- coulomb: float32 [128, 128, 128], P(None, 'grid'), may hold values from 0.1 to 10
Outputs:
- exchange: float32 [16, 2, 128, 128, 128], P('band', None, 'grid')
All inputs are finite; a program needn't handle non-finite values.
Results may differ from a plain program's by a relative error of at most 0.0001.
Values sent between devices are 32-bit elements; how exact they have to be, the bound alone decides.
No kernel may reach another device: no remote copies, remote signals or barrier semaphores. Data moves between devices by JAX's collectives and lax.ppermute only.
A program may use at most 64 MiB of HBM per device.

v0:
```python
import math
import jax
import jax.numpy as jnp
from jax import lax
from jax.sharding import PartitionSpec as P

NX = 128
NY = 128
NZ = 128
STEPS = 2
einsum_forms = {1: "pnbc,nk->pkbc", 2: "panc,nk->pakc", 3: "pabn,nk->pabk"}


def from_root(value, axis, source):
    kept = jnp.where(lax.axis_index(axis) == source, value, 0).astype(value.dtype)
    return lax.psum(kept, axis)


def dft_tables(length):
    indices = jnp.arange(length, dtype=jnp.int32)
    products = indices[:, None] * indices[None, :] % length
    angles = products.astype(jnp.float32) * (2.0 * math.pi / length)
    return (jnp.cos(angles), jnp.sin(angles))


def transform(real_part, imag_part, axis_dim, inverse):
    cosine, sine_table = dft_tables(real_part.shape[axis_dim])
    form = einsum_forms[axis_dim]

    def contract(values, table):
        return jnp.einsum(form, values, table, precision=lax.Precision.HIGHEST)

    re_cos = contract(real_part, cosine)
    re_sin = contract(real_part, sine_table)
    im_cos = contract(imag_part, cosine)
    im_sin = contract(imag_part, sine_table)
    if inverse:
        return (re_cos - im_sin, im_cos + re_sin)
    return (re_cos + im_sin, im_cos - re_sin)


def body(bands, coulomb):
    local = bands.shape[0]
    groups = lax.axis_size("band")
    kernel = coulomb * (1.0 / (NX * NY * NZ))
    own_re = bands[:, 0]
    own_im = bands[:, 1]
    totals = (jnp.zeros_like(own_re), jnp.zeros_like(own_im))
    for step_index in range(STEPS):
        owner = step_index * groups // STEPS
        visitors = from_root(bands, "band", owner)
        pair_vis_re = visitors[:, 0]
        pair_vis_im = visitors[:, 1]
        pair_real_part = pair_vis_re[None] * own_re[:, None] + pair_vis_im[None] * own_im[:, None]
        pair_imag_part = pair_vis_re[None] * own_im[:, None] - pair_vis_im[None] * own_re[:, None]
        pair_shape = (local * local,) + pair_real_part.shape[2:]
        real_part = pair_real_part.reshape(pair_shape)
        imag_part = pair_imag_part.reshape(pair_shape)
        potentials_real_part = real_part
        potentials_imag_part = imag_part
        potentials_real_part, potentials_imag_part = transform(
            potentials_real_part, potentials_imag_part, 3, False
        )
        potentials_real_part, potentials_imag_part = transform(
            potentials_real_part, potentials_imag_part, 2, False
        )
        stacked = jnp.stack([potentials_real_part, potentials_imag_part], axis=1)
        block = lax.all_to_all(stacked, "grid", split_axis=3, concat_axis=2, tiled=True)
        pencil_real_part, pencil_imag_part = transform(block[:, 0], block[:, 1], 1, False)
        pencil_real_part = pencil_real_part * kernel[None]
        pencil_imag_part = pencil_imag_part * kernel[None]
        pencil_real_part, pencil_imag_part = transform(pencil_real_part, pencil_imag_part, 1, True)
        back = jnp.stack([pencil_real_part, pencil_imag_part], axis=1)
        result = lax.all_to_all(back, "grid", split_axis=2, concat_axis=3, tiled=True)
        potentials_real_part, potentials_imag_part = transform(result[:, 0], result[:, 1], 2, True)
        pot_re, pot_im = transform(potentials_real_part, potentials_imag_part, 3, True)
        accumulate_pot_re = pot_re
        accumulate_pot_im = pot_im
        vis_re = visitors[:, 0][None]
        vis_im = visitors[:, 1][None]
        shape = (local, local) + accumulate_pot_re.shape[1:]
        accumulate_pot_re = accumulate_pot_re.reshape(shape)
        accumulate_pot_im = accumulate_pot_im.reshape(shape)
        add_re = jnp.sum(accumulate_pot_re * vis_re - accumulate_pot_im * vis_im, axis=1)
        add_im = jnp.sum(accumulate_pot_re * vis_im + accumulate_pot_im * vis_re, axis=1)
        totals = (totals[0] + add_re, totals[1] + add_im)
    return -0.25 * jnp.stack([totals[0], totals[1]], axis=1)


def solution(mesh):
    in_specs = (P("band", None, "grid", None, None), P(None, "grid", None))
    out_specs = P("band", None, "grid", None, None)
    return jax.shard_map(body, mesh=mesh, in_specs=in_specs, out_specs=out_specs, check_vma=False)
```

profile of v0, /device:TPU:24, one launch (start us, length us, event | category | flops | bytes accessed | tf_op | source)
XLA Modules:
  0.0 357.9 jit_solution(3360302418520842808)
XLA Ops:
  6.5 2.8 broadcast_select_fusion.1
  9.3 185.8 %all-reduce.3.cloned.1.call-done = (f32[1,2,8,128,128]{4,3,2,1,0:T(8,128)}, f32[1,2,8,128,128]{4,3,2,1,0:T(8,128)}) async-done(((f32[1,2,8,128,128]{4,3,2,1,0:T(8,128)}, f32[1,2,8,128,128]{4,3,2,1,0:T(8,128)}), (f32[1,2,8,128,128]{4,3,2,1,0:T(8,128)}, f32[1,2,8,128,128]{4,3,2,1,0:T(8,128)})) %all-reduce.3.cloned.1.call-update) | async-done | bytes 2097168 | tf_op jit(solution)/shard_map/psum | solution.py:16
  195.1 1.8 multiply_add_fusion.1
  201.9 0.9 fusion.18
  202.8 0.9 fusion.19
  203.8 1.6 copy.44
  205.3 5.6 %all-to-all-start = ((f32[1,2,8,128,128]{4,2,1,0,3:T(8,128)}), f32[1,2,8,128,128]{4,2,1,0,3:T(8,128)S(1)}, u32[]{:S(2)}, u32[]{:S(2)}) async-start(f32[1,2,8,128,128]{4,2,1,0,3:T(8,128)} %copy.44), calls=%async_computation | async-start | bytes 2097152 | tf_op jit(solution)/shard_map/all_to_all | solution.py:68
  215.1 0.9 fusion.9
  216.9 0.9 fusion.8
  217.9 1.6 copy.65
  219.4 19.5 %all-to-all-done = f32[1,2,8,128,128]{4,2,1,0,3:T(8,128)S(1)} async-done(((f32[1,2,8,128,128]{4,2,1,0,3:T(8,128)}), f32[1,2,8,128,128]{4,2,1,0,3:T(8,128)S(1)}, u32[]{:S(2)}, u32[]{:S(2)}) %all-to-all-start) | async-done | bytes 1048608 | tf_op jit(solution)/shard_map/all_to_all | solution.py:68
  238.9 3.8 %all-to-all-start.2 = ((f32[1,2,8,128,128]{4,2,1,0,3:T(8,128)}), f32[1,2,8,128,128]{4,2,1,0,3:T(8,128)S(1)}, u32[]{:S(2)}, u32[]{:S(2)}) async-start(f32[1,2,8,128,128]{4,2,1,0,3:T(8,128)} %copy.65), calls=%async_computation.2 | async-start | bytes 2097152 | tf_op jit(solution)/shard_map/all_to_all | solution.py:68
  244.8 0.9 fusion.16
  246.6 0.9 fusion.17
  247.5 0.9 fusion.14
  249.3 0.9 fusion.15
  250.3 1.6 copy.55
  251.8 20.1 %all-to-all-done.2 = f32[1,2,8,128,128]{4,2,1,0,3:T(8,128)S(1)} async-done(((f32[1,2,8,128,128]{4,2,1,0,3:T(8,128)}), f32[1,2,8,128,128]{4,2,1,0,3:T(8,128)S(1)}, u32[]{:S(2)}, u32[]{:S(2)}) %all-to-all-start.2) | async-done | bytes 1048608 | tf_op jit(solution)/shard_map/all_to_all | solution.py:68
  271.9 3.9 %all-to-all-start.1 = ((f32[1,2,128,8,128]{4,3,1,0,2:T(8,128)}), f32[1,2,128,8,128]{4,3,1,0,2:T(8,128)S(1)}, u32[]{:S(2)}, u32[]{:S(2)}) async-start(f32[1,2,128,8,128]{4,3,1,0,2:T(8,128)} %copy.55), calls=%async_computation.1 | async-start | bytes 2097152 | tf_op jit(solution)/shard_map/all_to_all | solution.py:74
  277.6 0.9 fusion.6
  279.4 0.9 fusion.7
  280.4 0.9 fusion.4
  282.1 0.9 fusion.5
  283.1 1.6 copy.75
  284.7 19.4 %all-to-all-done.1 = f32[1,2,128,8,128]{4,3,1,0,2:T(8,128)S(1)} async-done(((f32[1,2,128,8,128]{4,3,1,0,2:T(8,128)}), f32[1,2,128,8,128]{4,3,1,0,2:T(8,128)S(1)}, u32[]{:S(2)}, u32[]{:S(2)}) %all-to-all-start.1) | async-done | bytes 1048608 | tf_op jit(solution)/shard_map/all_to_all | solution.py:74
  304.1 4.6 %all-to-all-start.3 = ((f32[1,2,128,8,128]{4,3,1,0,2:T(8,128)}), f32[1,2,128,8,128]{4,3,1,0,2:T(8,128)}, u32[]{:S(2)}, u32[]{:S(2)}) async-start(f32[1,2,128,8,128]{4,3,1,0,2:T(8,128)} %copy.75), calls=%async_computation.3 | async-start | bytes 2097152 | tf_op jit(solution)/shard_map/all_to_all | solution.py:74
  310.5 25.1 %all-to-all-done.3 = f32[1,2,128,8,128]{4,3,1,0,2:T(8,128)} async-done(((f32[1,2,128,8,128]{4,3,1,0,2:T(8,128)}), f32[1,2,128,8,128]{4,3,1,0,2:T(8,128)}, u32[]{:S(2)}, u32[]{:S(2)}) %all-to-all-start.3) | async-done | bytes 1048608 | tf_op jit(solution)/shard_map/all_to_all | solution.py:74
  335.6 1.3 copy.158
  338.7 0.9 fusion.12
  345.4 0.9 fusion.3
  348.5 1.0 subtract_add_fusion
  349.5 1.1 maximum_multiply_fusion
  (50 shorter events, 29.0 us)
Async XLA Ops:
  6.5 188.6 %all-reduce.3.cloned.1.call-start = ((), (), s32[]{:S(2)}) async-start(), calls=%async_computation.4 | async-start | bytes 4194304 | tf_op jit(solution)/shard_map/psum | solution.py:16
  9.3 185.8 %copy-start.1 = (f32[1,2,8,128,128]{4,3,2,1,0:T(8,128)S(1)}, f32[1,2,8,128,128]{4,3,2,1,0:T(8,128)}, u32[]{:S(2)}) copy-start(f32[1,2,8,128,128]{4,3,2,1,0:T(8,128)} %param.2) | copy-start | bytes 3145732
  205.3 33.6 %all-to-all-start = ((f32[1,2,8,128,128]{4,2,1,0,3:T(8,128)}), f32[1,2,8,128,128]{4,2,1,0,3:T(8,128)S(1)}, u32[]{:S(2)}, u32[]{:S(2)}) async-start(f32[1,2,8,128,128]{4,2,1,0,3:T(8,128)} %copy.44), calls=%async_computation | async-start | bytes 2097152 | tf_op jit(solution)/shard_map/all_to_all | solution.py:68
  238.9 33.0 %all-to-all-start.2 = ((f32[1,2,8,128,128]{4,2,1,0,3:T(8,128)}), f32[1,2,8,128,128]{4,2,1,0,3:T(8,128)S(1)}, u32[]{:S(2)}, u32[]{:S(2)}) async-start(f32[1,2,8,128,128]{4,2,1,0,3:T(8,128)} %copy.65), calls=%async_computation.2 | async-start | bytes 2097152 | tf_op jit(solution)/shard_map/all_to_all | solution.py:68
  243.8 1.0 copy-start
  271.9 32.2 %all-to-all-start.1 = ((f32[1,2,128,8,128]{4,3,1,0,2:T(8,128)}), f32[1,2,128,8,128]{4,3,1,0,2:T(8,128)S(1)}, u32[]{:S(2)}, u32[]{:S(2)}) async-start(f32[1,2,128,8,128]{4,3,1,0,2:T(8,128)} %copy.55), calls=%async_computation.1 | async-start | bytes 2097152 | tf_op jit(solution)/shard_map/all_to_all | solution.py:74
  304.1 31.6 %all-to-all-start.3 = ((f32[1,2,128,8,128]{4,3,1,0,2:T(8,128)}), f32[1,2,128,8,128]{4,3,1,0,2:T(8,128)}, u32[]{:S(2)}, u32[]{:S(2)}) async-start(f32[1,2,128,8,128]{4,3,1,0,2:T(8,128)} %copy.75), calls=%async_computation.3 | async-start | bytes 2097152 | tf_op jit(solution)/shard_map/all_to_all | solution.py:74
  346.3 1.7 copy-start.3
  347.2 1.3 copy-start.2
Sparse Core Ops, SparseCore 0:
  10.0 185.0 all-reduce.2
where the time goes:
time: 364 us; the launch traced here: 358 us
  waiting for transfers between devices  270 us (74%)
  matrix products  41.2 us (11%)
  starting transfers between devices  17.9 us (5%)
  between operations  14.3 us (4%)
  local copies, waits for them, and re-layouts  8.56 us (2%)
  other arithmetic  5.95 us (2%)
    psum x1, waiting for transfers between devices, from_root(): return lax.psum(kept, axis)  186 us
    all_to_all x2, waiting for transfers between devices, body(): lax.all_to_all(back, 'grid', split_axis=2, concat_axis=3, tiled=True)  44.5 us
    dot_general x48, matrix products, contract(): return jnp.einsum(form, values, table, precision=lax.Precision.HIGHEST)  41.2 us
    all_to_all x2, waiting for transfers between devices, body(): lax.all_to_all(stacked, 'grid', split_axis=3, concat_axis=2, tiled=True)  39.6 us
    all_to_all x2, starting transfers between devices, body(): lax.all_to_all(stacked, 'grid', split_axis=3, concat_axis=2, tiled=True)  9.45 us
    all_to_all x2, starting transfers between devices, body(): lax.all_to_all(back, 'grid', split_axis=2, concat_axis=3, tiled=True)  8.46 us
  transfers between devices with their start and end apart: 5, of which 5 were waited for; matrix products, arithmetic and copies ran while one was open for 8% of the time, Pallas kernels for 0%

commit v1 on v0

--- a/solution.py
+++ b/solution.py
@@ -13,7 +13,7 @@
 
 def from_root(value, axis, source):
     kept = jnp.where(lax.axis_index(axis) == source, value, 0).astype(value.dtype)
-    return lax.psum(kept, axis)
+    return jnp.sum(lax.all_gather(kept, axis), axis=0)
 
 
 def dft_tables(length):

time: 364 us -> 538 us (1.48)
  the two profiles are of different devices: /device:TPU:24 before, /device:TPU:1 now
where the time goes in v1:
time: 538 us; the launch traced here: 529 us
  waiting for transfers between devices  416 us (77%)
  matrix products  47 us (9%)
  other arithmetic  21.3 us (4%)
  starting transfers between devices  18.6 us (3%)
  between operations  14.3 us (3%)
  local copies, waits for them, and re-layouts  11.7 us (2%)
    all_gather x2, waiting for transfers between devices, from_root(): return jnp.sum(lax.all_gather(kept, axis), axis=0)  342 us
    dot_general x48, matrix products, contract(): return jnp.einsum(form, values, table, precision=lax.Precision.HIGHEST)  47 us
    all_to_all x2, waiting for transfers between devices, body(): lax.all_to_all(back, 'grid', split_axis=2, concat_axis=3, tiled=True)  39.2 us
    all_to_all x2, waiting for transfers between devices, body(): lax.all_to_all(stacked, 'grid', split_axis=3, concat_axis=2, tiled=True)  33.6 us
    reduce_sum x2, other arithmetic, from_root(): return jnp.sum(lax.all_gather(kept, axis), axis=0)  14.8 us
  transfers between devices with their start and end apart: 6, of which 6 were waited for; matrix products, arithmetic and copies ran while one was open for 8% of the time, Pallas kernels for 0%

profile of v1, /device:TPU:1, one launch (start us, length us, event | category | flops | bytes accessed | tf_op | source)
XLA Modules:
  0.0 528.8 jit_solution(11364402719707791951)
XLA Ops:
  6.5 2.8 broadcast_select_fusion.1
  10.1 178.4 %all-gather.5.cloned.1.call-done = f32[16,2,8,128,128]{4,3,2,1,0:T(8,128)} async-done(((f32[1,2,8,128,128]{4,3,2,1,0:T(8,128)}), f32[16,2,8,128,128]{4,3,2,1,0:T(8,128)}) %all-gather.5.cloned.1.call-update) | async-done | bytes 16777232 | tf_op jit(solution)/shard_map/all_gather | solution.py:16
  188.5 7.4 %reduce.2 = f32[2,8,128,128]{3,2,1,0:T(8,128)S(1)} reduce(f32[16,2,8,128,128]{4,3,2,1,0:T(8,128)} %all-gather.5.cloned.1.call-done, f32[]{:T(128)} %constant.61.clone.1), dimensions={0}, to_apply=%region_0.1 | reduce | flops 3932160 | bytes 17825796 | tf_op jit(solution)/shard_map/reduce_sum | solution.py:16
  195.9 164.0 %all-gather.7.cloned.1.call-done = f32[16,2,8,128,128]{4,3,2,1,0:T(8,128)} async-done(((f32[1,2,8,128,128]{4,3,2,1,0:T(8,128)}), f32[16,2,8,128,128]{4,3,2,1,0:T(8,128)}) %all-gather.7.cloned.1.call-update) | async-done | bytes 16777232 | tf_op jit(solution)/shard_map/all_gather | solution.py:16
  359.9 7.4 %reduce.3 = f32[2,8,128,128]{3,2,1,0:T(8,128)S(1)} reduce(f32[16,2,8,128,128]{4,3,2,1,0:T(8,128)} %all-gather.7.cloned.1.call-done, f32[]{:T(128)} %constant.61.clone.1), dimensions={0}, to_apply=%region_1.2 | reduce | flops 3932160 | bytes 17825796 | tf_op jit(solution)/shard_map/reduce_sum | solution.py:16
  367.3 2.3 multiply_add_fusion.1
  376.5 1.6 copy.44
  378.1 4.8 all-to-all-start
  382.9 1.9 fusion.20
  385.6 1.9 convolution_add_fusion.5
  391.9 1.6 copy.65
  393.5 16.7 %all-to-all-done = f32[1,2,8,128,128]{4,2,1,0,3:T(8,128)} async-done(((f32[1,2,8,128,128]{4,2,1,0,3:T(8,128)}), f32[1,2,8,128,128]{4,2,1,0,3:T(8,128)}, u32[]{:S(2)}, u32[]{:S(2)}) %all-to-all-start) | async-done | bytes 1048608 | tf_op jit(solution)/shard_map/all_to_all | solution.py:68
  410.2 4.5 all-to-all-start.2
  414.7 1.3 copy.161
  417.8 0.9 fusion.16
  423.2 1.6 copy.55
  424.8 16.9 %all-to-all-done.2 = f32[1,2,8,128,128]{4,2,1,0,3:T(8,128)} async-done(((f32[1,2,8,128,128]{4,2,1,0,3:T(8,128)}), f32[1,2,8,128,128]{4,2,1,0,3:T(8,128)}, u32[]{:S(2)}, u32[]{:S(2)}) %all-to-all-start.2) | async-done | bytes 1048608 | tf_op jit(solution)/shard_map/all_to_all | solution.py:68
  441.7 4.6 all-to-all-start.1
  446.3 1.3 copy.159
  449.4 0.9 fusion.6
  454.9 1.6 copy.75
  456.5 17.0 %all-to-all-done.1 = f32[1,2,128,8,128]{4,3,1,0,2:T(8,128)} async-done(((f32[1,2,128,8,128]{4,3,1,0,2:T(8,128)}), f32[1,2,128,8,128]{4,3,1,0,2:T(8,128)}, u32[]{:S(2)}, u32[]{:S(2)}) %all-to-all-start.1) | async-done | bytes 1048608 | tf_op jit(solution)/shard_map/all_to_all | solution.py:74
  473.4 4.7 all-to-all-start.3
  478.1 1.3 copy.160
  479.4 1.7 fusion.35
  481.1 1.7 fusion.34
  482.7 22.2 %all-to-all-done.3 = f32[1,2,128,8,128]{4,3,1,0,2:T(8,128)} async-done(((f32[1,2,128,8,128]{4,3,1,0,2:T(8,128)}), f32[1,2,128,8,128]{4,3,1,0,2:T(8,128)}, u32[]{:S(2)}, u32[]{:S(2)}) %all-to-all-start.3) | async-done | bytes 1048608 | tf_op jit(solution)/shard_map/all_to_all | solution.py:74
  504.9 1.3 copy.158
  508.0 1.9 fusion.12
  510.7 1.9 fusion.13
  519.4 1.1 subtract_add_fusion
  520.5 1.1 maximum_multiply_fusion
  (49 shorter events, 34.3 us)
Async XLA Ops:
  6.5 182.0 %all-gather.5.cloned.1.call-start = ((), (), s32[]{:S(2)}) async-start(), calls=%async_computation.4 | async-start | bytes 17825792 | tf_op jit(solution)/shard_map/all_gather | solution.py:16
  9.4 350.6 %all-gather.7.cloned.1.call-start = ((), (), s32[]{:S(2)}) async-start(), calls=%async_computation.5 | async-start | bytes 17825792 | tf_op jit(solution)/shard_map/all_gather | solution.py:16
  372.1 45.7 %copy-start = (f32[128,8,128]{2,1,0:T(8,128)S(1)}, f32[128,8,128]{2,1,0:T(8,128)}, u32[]{:S(2)}) copy-start(f32[128,8,128]{2,1,0:T(8,128)} %param.3) | copy-start | bytes 1572868
  378.1 32.0 %all-to-all-start = ((f32[1,2,8,128,128]{4,2,1,0,3:T(8,128)}), f32[1,2,8,128,128]{4,2,1,0,3:T(8,128)}, u32[]{:S(2)}, u32[]{:S(2)}) async-start(f32[1,2,8,128,128]{4,2,1,0,3:T(8,128)} %copy.44), calls=%async_computation | async-start | bytes 2097152 | tf_op jit(solution)/shard_map/all_to_all | solution.py:68
  410.2 31.6 %all-to-all-start.2 = ((f32[1,2,8,128,128]{4,2,1,0,3:T(8,128)}), f32[1,2,8,128,128]{4,2,1,0,3:T(8,128)}, u32[]{:S(2)}, u32[]{:S(2)}) async-start(f32[1,2,8,128,128]{4,2,1,0,3:T(8,128)} %copy.65), calls=%async_computation.2 | async-start | bytes 2097152 | tf_op jit(solution)/shard_map/all_to_all | solution.py:68
  441.7 31.7 %all-to-all-start.1 = ((f32[1,2,128,8,128]{4,3,1,0,2:T(8,128)}), f32[1,2,128,8,128]{4,3,1,0,2:T(8,128)}, u32[]{:S(2)}, u32[]{:S(2)}) async-start(f32[1,2,128,8,128]{4,3,1,0,2:T(8,128)} %copy.55), calls=%async_computation.1 | async-start | bytes 2097152 | tf_op jit(solution)/shard_map/all_to_all | solution.py:74
  473.4 31.5 %all-to-all-start.3 = ((f32[1,2,128,8,128]{4,3,1,0,2:T(8,128)}), f32[1,2,128,8,128]{4,3,1,0,2:T(8,128)}, u32[]{:S(2)}, u32[]{:S(2)}) async-start(f32[1,2,128,8,128]{4,3,1,0,2:T(8,128)} %copy.75), calls=%async_computation.3 | async-start | bytes 2097152 | tf_op jit(solution)/shard_map/all_to_all | solution.py:74
Sparse Core Ops, SparseCore 0:
  10.1 178.4 all-gather.4
  191.3 168.6 all-gather.6
